TPU v7x, 512 devices: a whole 4x4x16 slice. The times are simulated.
512 devices in a mesh: band: 256 (over x_hi, y, z, core), pair: 2 (over x_lo).
Axes of the slice: x: 4 (x_hi: 2, x_lo: 2; x = x_hi * 2 + x_lo), y: 4, z: 16, core: 2. Of those that a mesh axis runs over, the one named last changes fastest.
Arguments:
- frame1: bfloat16 [256, 768, 256], P('band', 'pair'), parts along dimension 1, may hold values from -6 to 6, as said below
- frame2: bfloat16 [256, 768, 256], P('band', 'pair'), parts along dimension 1, may hold values from -6 to 6, as said below
- context: bfloat16 [256, 768, 128], P('band', 'pair'), parts along dimension 1, may hold values from -6 to 6
- hidden_init: bfloat16 [256, 768, 128], P('band', 'pair'), parts along dimension 1, may hold values from -1 to 1
- offsets: int32 [2, 256, 768], P(None, 'band', 'pair'), parts along dimension 2, may hold values from -4 to 4
- w_motion: float32 [3, 128], replicated, may hold values from -3.5 to 3.5
- w_row: bfloat16 [5, 384, 384], replicated, may hold values from -0.125 to 0.125
- w_col: bfloat16 [5, 384, 384], replicated, may hold values from -0.125 to 0.125
Outputs:
- hidden: float32 [256, 768, 128], P('band', 'pair'), parts along dimension 1
- flow: float32 [2, 256, 768], P(None, 'band', 'pair'), parts along dimension 2
There are 2 independent parts, one for each index of `pair`. A program takes and returns all parts, laid end to end along the dimension named above; an argument that names none is the same for every part. Nothing has to cross between parts.
Inputs may be any that keep to these rules, and one draw needn't show every extreme that they name: `frame1`: feature vectors. `frame2`: feature vectors. offsets[0] and offsets[1] are each pixel's teacher lookup offsets, in rows and in strips.
All inputs are finite; a program needn't handle non-finite values.
Results may differ from a plain program's by a relative error of at most 0.0041.
Values may be sent and summed in bfloat16 or wider, within the bound.
No kernel may reach another device: no remote copies, remote signals or barrier semaphores. Data moves between devices by JAX's collectives and lax.ppermute only.
A program may use at most 64 MiB of HBM per device.

v0:
```python
import math
import jax
import jax.numpy as jnp
from jax import lax
from jax.sharding import PartitionSpec as P

ITERS = 2


def passed_along(array, axis, by):
    count = lax.axis_size(axis)
    pairs = [(i, i + by) for i in range(count) if 0 <= i + by < count]
    return lax.ppermute(array, axis, pairs)


def pool_strips(frame2):
    band_rows, image_width, channels = frame2.shape
    blocks = frame2.astype(jnp.float32).reshape(band_rows, image_width // 8, 8, channels)
    return (jnp.sum(blocks, axis=2) / 2.0).astype(jnp.bfloat16)


def lookup_targets(offsets, row_first, total_rows, image_width):
    band_rows = offsets.shape[1]
    pixel_row = (
        row_first
        + jnp.arange(band_rows, dtype=jnp.int32)[:, None]
        + jnp.zeros((1, image_width), jnp.int32)
    )
    pixel_col = jnp.arange(image_width, dtype=jnp.int32)[None, :]
    target_row = pixel_row + offsets[0]
    target_col = pixel_col // 8 + offsets[1]
    inside = (
        (target_row >= 0)
        & (target_row < total_rows)
        & (target_col >= 0)
        & (target_col < image_width // 8)
    )
    target_row = jnp.where(inside, target_row, -1)
    target_col = jnp.where(inside, target_col, -1)
    return (target_row, target_col, pixel_row, pixel_col)


def strip_step(
    state, feature_rows, strip_block, row_zero, total_rows, image_width, target_row, target_col
):
    block_rows, grid_cols, channels = strip_block.shape
    scores = jnp.dot(
        feature_rows,
        strip_block.reshape(block_rows * grid_cols, channels).T,
        preferred_element_type=jnp.float32,
    ) / math.sqrt(channels)
    running_max, denominator, acc_row, acc_col, lookup = state
    new_max = jnp.maximum(running_max, jnp.max(scores, axis=1))
    shrink = jnp.exp(running_max - new_max)
    exponent = jnp.exp(scores - new_max[:, None]).reshape(-1, block_rows, grid_cols)
    strip_row = row_zero + jnp.arange(block_rows, dtype=jnp.int32)
    column_ids = jnp.arange(grid_cols, dtype=jnp.int32)
    row_centre = strip_row.astype(jnp.float32) / total_rows
    col_centre = ((8 * column_ids).astype(jnp.float32) + 3.5) / image_width
    row_weight = jnp.sum(exponent, axis=2)
    col_weight = jnp.sum(exponent, axis=1)
    scores_grid = scores.reshape(-1, block_rows, grid_cols)
    hit = (strip_row[None, :, None] == target_row[:, None, None]) & (
        column_ids[None, None, :] == target_col[:, None, None]
    )
    found = jnp.sum(jnp.where(hit, scores_grid, 0.0), axis=(1, 2))
    return (
        new_max,
        denominator * shrink + jnp.sum(row_weight, axis=1),
        acc_row * shrink + jnp.sum(row_weight * row_centre[None, :], axis=1),
        acc_col * shrink + jnp.sum(col_weight * col_centre[None, :], axis=1),
        lookup + found,
    )


def conv_valid(source, weight, conv_axis):
    out_count = source.shape[conv_axis] - 4
    summed = None
    for kernel_tap in range(5):
        tap_slice = lax.slice_in_dim(source, kernel_tap, kernel_tap + out_count, axis=conv_axis)
        tap_term = jnp.dot(
            tap_slice.reshape(-1, tap_slice.shape[-1]),
            weight[kernel_tap],
            preferred_element_type=jnp.float32,
        )
        summed = tap_term if summed is None else summed + tap_term
    out_shape = tuple(tap_slice.shape[:-1]) + (weight.shape[-1],)
    return summed.reshape(out_shape)


def pad_columns(source):
    return jnp.pad(source, ((0, 0), (2, 2), (0, 0)))


def rows_around(source, depth, mover):
    above = [
        mover(source, offset)
        for offset in list(range(depth, 0, -1)) + list(range(-1, -depth - 1, -1))
    ]
    return jnp.concatenate(above[:depth] + [source] + above[depth:], axis=0)


def row_pass(hidden, from_inputs, weight):
    width_h = hidden.shape[-1]
    hidden_half = lax.optimization_barrier(hidden.astype(jnp.bfloat16))
    gate_pair = jax.nn.sigmoid(
        conv_valid(pad_columns(hidden_half), weight[:, :width_h, : 2 * width_h], 1)
        + from_inputs[..., : 2 * width_h]
    )
    update_gate = gate_pair[..., :width_h]
    reset_gate = gate_pair[..., width_h:]
    gated = (reset_gate * hidden_half.astype(jnp.float32)).astype(jnp.bfloat16)
    candidate = jnp.tanh(
        conv_valid(pad_columns(gated), weight[:, :width_h, 2 * width_h :], 1)
        + from_inputs[..., 2 * width_h :]
    )
    return (1.0 - update_gate) * hidden + update_gate * candidate


def column_pass_each(hidden, from_inputs, weight):
    width_h = hidden.shape[-1]
    hidden_half = lax.optimization_barrier(hidden.astype(jnp.bfloat16))
    hidden_ext = rows_around(
        hidden_half, 2, lambda source, offset: passed_along(source, "band", offset)
    )
    gate_pair = jax.nn.sigmoid(
        conv_valid(hidden_ext, weight[:, :width_h, : 2 * width_h], 0)
        + from_inputs[..., : 2 * width_h]
    )
    update_gate = gate_pair[..., :width_h]
    reset_gate = gate_pair[..., width_h:]
    gated = (reset_gate * hidden_half.astype(jnp.float32)).astype(jnp.bfloat16)
    gated_ext = rows_around(gated, 2, lambda source, offset: passed_along(source, "band", offset))
    candidate = jnp.tanh(
        conv_valid(gated_ext, weight[:, :width_h, 2 * width_h :], 0)
        + from_inputs[..., 2 * width_h :]
    )
    return (1.0 - update_gate) * hidden + update_gate * candidate


def per_device(frame1, frame2, context, hidden_init, offsets, w_motion, w_row, w_col):
    band_rows, image_width, channels = frame1.shape
    total_rows = band_rows * lax.axis_size("band")
    row_first = lax.axis_index("band") * band_rows
    strips = pool_strips(frame2)
    target_row, target_col, pixel_row, pixel_col = lookup_targets(
        offsets, row_first, total_rows, image_width
    )
    pixel_count = band_rows * image_width
    features = frame1.reshape(pixel_count, channels)
    rows_target = target_row.reshape(pixel_count)
    cols_target = target_col.reshape(pixel_count)
    zeros_state = jnp.zeros((pixel_count,), jnp.float32)
    initial = (
        jnp.full((pixel_count,), -jnp.inf, jnp.float32),
        zeros_state,
        zeros_state,
        zeros_state,
        zeros_state,
    )
    state = initial
    arriving = lax.all_gather(strips, "band", axis=0, tiled=True)
    arriving_rows = arriving.shape[0]
    step_rows = min(arriving_rows, 16)
    full_steps = arriving_rows // step_rows
    blocks = arriving.reshape((full_steps, step_rows) + arriving.shape[1:])
    starts = step_rows * jnp.arange(full_steps, dtype=jnp.int32)

    def advance(carry, pieces):
        return (
            strip_step(
                carry,
                features,
                pieces[0],
                pieces[1],
                total_rows,
                image_width,
                rows_target,
                cols_target,
            ),
            None,
        )

    state, unused = lax.scan(advance, state, (blocks, starts))
    running_max, denominator, acc_row, acc_col, lookup = state
    flow_row = (acc_row / denominator).reshape(band_rows, image_width) - pixel_row.astype(
        jnp.float32
    ) / total_rows
    flow_col = (acc_col / denominator).reshape(band_rows, image_width) - pixel_col.astype(
        jnp.float32
    ) / image_width
    lookup = lookup.reshape(band_rows, image_width)
    motion = jax.nn.relu(
        flow_row[..., None] * w_motion[0]
        + flow_col[..., None] * w_motion[1]
        + lookup[..., None] * w_motion[2]
    ).astype(jnp.bfloat16)
    inputs = jnp.concatenate([context, motion], axis=-1)
    width_h = hidden_init.shape[-1]
    from_row = conv_valid(pad_columns(inputs), w_row[:, width_h:, :], 1)
    hidden = hidden_init.astype(jnp.float32)
    inputs_ext = rows_around(inputs, 2, lambda source, offset: passed_along(source, "band", offset))
    from_col = conv_valid(inputs_ext, w_col[:, width_h:, :], 0)
    for iteration in range(ITERS):
        hidden = row_pass(hidden, from_row, w_row)
        hidden = column_pass_each(hidden, from_col, w_col)
    return (hidden, jnp.stack([flow_row, flow_col]))


def solution(mesh):
    return jax.shard_map(
        per_device,
        mesh=mesh,
        in_specs=(
            P("band", "pair", None),
            P("band", "pair", None),
            P("band", "pair", None),
            P("band", "pair", None),
            P(None, "band", "pair"),
            P(),
            P(),
            P(),
        ),
        out_specs=(P("band", "pair", None), P(None, "band", "pair")),
        check_vma=False,
    )
```

profile of v0, /device:TPU:7, one launch (start us, length us, event | category | flops | bytes accessed | tf_op | source)
XLA Modules:
  0.0 416.5 jit_solution(839724236668119955)
XLA Ops:
  7.2 1.2 convert_reduce_fusion
  9.1 0.8 slice_bitcast_fusion.2
  11.3 1.1 fusion.158
  12.4 1.1 convolution_add_fusion.17
  14.0 222.3 %all-gather.3.cloned.1.call-done = bf16[12288,256]{1,0:T(8,128)(2,1)} async-done(((bf16[48,256]{1,0:T(8,128)(2,1)}), bf16[12288,256]{1,0:T(8,128)(2,1)}) %all-gather.3.cloned.1.call-update) | async-done | bytes 6291472 | tf_op jit(solution)/shard_map/all_gather | solution.py:162
  236.2 70.1 %while.19 = (s32[]{:T(128)}, f32[384]{0:T(512)S(1)}, f32[384]{0:T(512)S(1)}, f32[384]{0:T(512)S(1)}, f32[384]{0:T(512)S(1)}, /*index=5*/f32[384]{0:T(512)S(1)}, ...) while((s32[]{:T(128)}, f32[384]{0:T(512)S(1)}, ...), condition=%wide.region_9.10_spmd.clone, body=%wide.region_1.9_spmd.clone.sunk | while | flops 153702400 | bytes 6978856 | solution.py:184
  236.2 1.1 constant_dynamic-slice_fusion.2
  240.6 1.0 constant_dynamic-slice_fusion.2
  245.0 1.0 constant_dynamic-slice_fusion.2
  249.4 1.0 constant_dynamic-slice_fusion.2
  253.8 1.0 constant_dynamic-slice_fusion.2
  258.2 1.0 constant_dynamic-slice_fusion.2
  262.5 1.0 constant_dynamic-slice_fusion.2
  266.9 1.0 constant_dynamic-slice_fusion.2
  271.3 1.0 constant_dynamic-slice_fusion.2
  275.7 1.0 constant_dynamic-slice_fusion.2
  280.1 1.0 constant_dynamic-slice_fusion.2
  284.4 1.0 constant_dynamic-slice_fusion.2
  288.8 1.0 constant_dynamic-slice_fusion.2
  293.2 1.0 constant_dynamic-slice_fusion.2
  297.6 1.0 constant_dynamic-slice_fusion.2
  302.0 1.0 constant_dynamic-slice_fusion.2
  309.2 3.3 collective-permute-start.1
  312.5 2.2 collective-permute-start
  314.7 8.8 %collective-permute-start.3 = (bf16[1,384,128]{2,1,0:T(8,128)(2,1)S(1)}, bf16[1,384,128]{2,1,0:T(8,128)(2,1)S(1)}, u32[]{:S(2)}, u32[]{:S(2)}) collective-permute-start(bf16[1,384,128]{2,1,0:T(8,128)(2,1)S(1)} %get-tuple-element.142), channel_id=1, source_target_pairs={{4,0},{6,2},{8,4},{10,6},{12,8},{14,10},{16,12},{18,14},{20,16},{2... | collective-permute-start | bytes 294920 | tf_op jit(solution)/shard_map/ppermute | solution.py:13
  323.5 1.9 collective-permute-start.2
  325.4 3.6 collective-permute-start.5
  330.1 1.9 collective-permute-start.4
  332.3 9.1 %collective-permute-start.7 = (bf16[1,384,256]{2,1,0:T(8,128)(2,1)S(1)}, bf16[1,384,256]{2,1,0:T(8,128)(2,1)S(1)}, u32[]{:S(2)}, u32[]{:S(2)}) collective-permute-start(bf16[1,384,256]{2,1,0:T(8,128)(2,1)S(1)} %pad_maximum_fusion), channel_id=1, source_target_pairs={{4,0},{6,2},{8,4},{10,6},{12,8},{14,10},{16,12},{18,14},{20,16},{2... | collective-permute-start | bytes 589832 | tf_op jit(solution)/shard_map/ppermute | solution.py:13
  341.6 1.9 collective-permute-start.6
  344.2 1.8 collective-permute-done.7
  346.3 2.2 collective-permute-done.6
  349.1 1.9 collective-permute-start.9
  351.2 1.9 collective-permute-start.8
  353.1 9.1 %collective-permute-start.11 = (bf16[1,384,128]{2,1,0:T(8,128)(2,1)S(1)}, bf16[1,384,128]{2,1,0:T(8,128)(2,1)S(1)}, u32[]{:S(2)}, u32[]{:S(2)}) collective-permute-start(bf16[1,384,128]{2,1,0:T(8,128)(2,1)S(1)} %fusion.60), channel_id=1, source_target_pairs={{4,0},{6,2},{8,4},{10,6},{12,8},{14,10},{16,12},{18,14},{20,16},{2... | collective-permute-start | bytes 294920 | tf_op jit(solution)/shard_map/ppermute | solution.py:13
  362.2 3.0 collective-permute-start.10
  365.7 2.5 collective-permute-done.10
  370.3 1.9 collective-permute-start.13
  372.5 1.9 collective-permute-start.12
  374.4 9.1 %collective-permute-start.15 = (bf16[1,384,128]{2,1,0:T(8,128)(2,1)S(1)}, bf16[1,384,128]{2,1,0:T(8,128)(2,1)S(1)}, u32[]{:S(2)}, u32[]{:S(2)}) collective-permute-start(bf16[1,384,128]{2,1,0:T(8,128)(2,1)S(1)} %get-tuple-element.146), channel_id=1, source_target_pairs={{4,0},{6,2},{8,4},{10,6},{12,8},{14,10},{16,12},{18,14},{20,16},{2... | collective-permute-start | bytes 294920 | tf_op jit(solution)/shard_map/ppermute | solution.py:13
  383.5 3.0 collective-permute-start.14
  387.1 2.3 collective-permute-done.14
  389.7 1.9 collective-permute-start.17
  391.8 1.9 collective-permute-start.16
  393.7 9.1 %collective-permute-start.19 = (bf16[1,384,128]{2,1,0:T(8,128)(2,1)S(1)}, bf16[1,384,128]{2,1,0:T(8,128)(2,1)S(1)}, u32[]{:S(2)}, u32[]{:S(2)}) collective-permute-start(bf16[1,384,128]{2,1,0:T(8,128)(2,1)S(1)} %fusion.58), channel_id=1, source_target_pairs={{4,0},{6,2},{8,4},{10,6},{12,8},{14,10},{16,12},{18,14},{20,16},{2... | collective-permute-start | bytes 294920 | tf_op jit(solution)/shard_map/ppermute | solution.py:13
  402.8 3.0 collective-permute-start.18
  406.3 2.4 collective-permute-done.18
  408.8 0.9 multiply_add_fusion
  (365 shorter events, 65.1 us)
Async XLA Ops:
  7.2 6.4 %copy-start.1 = (bf16[1,384,128]{2,1,0:T(8,128)(2,1)S(1)}, bf16[1,384,128]{2,1,0:T(8,128)(2,1)}, u32[]{:S(2)}) copy-start(bf16[1,384,128]{2,1,0:T(8,128)(2,1)} %param.13) | copy-start | bytes 294916
  7.2 6.4 %copy-start.3 = (bf16[5,384,384]{2,1,0:T(8,128)(2,1)S(1)}, bf16[5,384,384]{2,1,0:T(8,128)(2,1)}, u32[]{:S(2)}) copy-start(bf16[5,384,384]{2,1,0:T(8,128)(2,1)} %param.16) | copy-start | bytes 4423684
  7.2 229.0 %all-gather.3.cloned.1.call-start = ((), (), s32[]{:S(2)}) async-start(), calls=%async_computation | async-start | bytes 6316032 | tf_op jit(solution)/shard_map/all_gather | solution.py:162
  12.4 223.8 %copy-start = (bf16[1,384,256]{2,1,0:T(8,128)(2,1)S(1)}, bf16[1,384,256]{2,1,0:T(8,128)(2,1)}, u32[]{:S(2)}) copy-start(bf16[1,384,256]{2,1,0:T(8,128)(2,1)} %param.10) | copy-start | bytes 589828
  236.2 70.3 %copy-start.4 = (bf16[1,384,128]{2,1,0:T(8,128)(2,1)S(1)}, bf16[1,384,128]{2,1,0:T(8,128)(2,1)}, u32[]{:S(2)}) copy-start(bf16[1,384,128]{2,1,0:T(8,128)(2,1)} %param.12) | copy-start | bytes 294916
  308.3 20.8 %copy-start.2 = (bf16[5,384,384]{2,1,0:T(8,128)(2,1)S(1)}, bf16[5,384,384]{2,1,0:T(8,128)(2,1)}, u32[]{:S(2)}) copy-start(bf16[5,384,384]{2,1,0:T(8,128)(2,1)} %param.17) | copy-start | bytes 4423684
  309.2 21.0 %collective-permute-start.1 = (bf16[1,384,128]{2,1,0:T(8,128)(2,1)S(1)}, bf16[1,384,128]{2,1,0:T(8,128)(2,1)S(1)}, u32[]{:S(2)}, u32[]{:S(2)}) collective-permute-start(bf16[1,384,128]{2,1,0:T(8,128)(2,1)S(1)} %get-tuple-element.142), channel_id=1, source_target_pairs={{0,2},{2,4},{4,6},{6,8},{8,10},{10,12},{12,14},{14,16},{16,18},{18... | collective-permute-start | bytes 294920 | tf_op jit(solution)/shard_map/ppermute | solution.py:13
  312.5 19.8 %collective-permute-start = (bf16[1,384,128]{2,1,0:T(8,128)(2,1)S(1)}, bf16[1,384,128]{2,1,0:T(8,128)(2,1)S(1)}, u32[]{:S(2)}, u32[]{:S(2)}) collective-permute-start(bf16[1,384,128]{2,1,0:T(8,128)(2,1)S(1)} %get-tuple-element.142), channel_id=1, source_target_pairs={{0,4},{2,6},{4,8},{6,10},{8,12},{10,14},{12,16},{14,18},{16,20},{1... | collective-permute-start | bytes 294920 | tf_op jit(solution)/shard_map/ppermute | solution.py:13
  314.7 26.8 %collective-permute-start.3 = (bf16[1,384,128]{2,1,0:T(8,128)(2,1)S(1)}, bf16[1,384,128]{2,1,0:T(8,128)(2,1)S(1)}, u32[]{:S(2)}, u32[]{:S(2)}) collective-permute-start(bf16[1,384,128]{2,1,0:T(8,128)(2,1)S(1)} %get-tuple-element.142), channel_id=1, source_target_pairs={{4,0},{6,2},{8,4},{10,6},{12,8},{14,10},{16,12},{18,14},{20,16},{2... | collective-permute-start | bytes 294920 | tf_op jit(solution)/shard_map/ppermute | solution.py:13
  323.5 25.3 %collective-permute-start.2 = (bf16[1,384,128]{2,1,0:T(8,128)(2,1)S(1)}, bf16[1,384,128]{2,1,0:T(8,128)(2,1)S(1)}, u32[]{:S(2)}, u32[]{:S(2)}) collective-permute-start(bf16[1,384,128]{2,1,0:T(8,128)(2,1)S(1)} %get-tuple-element.142), channel_id=1, source_target_pairs={{2,0},{4,2},{6,4},{8,6},{10,8},{12,10},{14,12},{16,14},{18,16},{20... | collective-permute-start | bytes 294920 | tf_op jit(solution)/shard_map/ppermute | solution.py:13
  325.4 18.3 %collective-permute-start.5 = (bf16[1,384,256]{2,1,0:T(8,128)(2,1)S(1)}, bf16[1,384,256]{2,1,0:T(8,128)(2,1)S(1)}, u32[]{:S(2)}, u32[]{:S(2)}) collective-permute-start(bf16[1,384,256]{2,1,0:T(8,128)(2,1)S(1)} %pad_maximum_fusion), channel_id=1, source_target_pairs={{0,2},{2,4},{4,6},{6,8},{8,10},{10,12},{12,14},{14,16},{16,18},{18... | collective-permute-start | bytes 589832 | tf_op jit(solution)/shard_map/ppermute | solution.py:13
  330.1 13.8 %collective-permute-start.4 = (bf16[1,384,256]{2,1,0:T(8,128)(2,1)S(1)}, bf16[1,384,256]{2,1,0:T(8,128)(2,1)S(1)}, u32[]{:S(2)}, u32[]{:S(2)}) collective-permute-start(bf16[1,384,256]{2,1,0:T(8,128)(2,1)S(1)} %pad_maximum_fusion), channel_id=1, source_target_pairs={{0,4},{2,6},{4,8},{6,10},{8,12},{10,14},{12,16},{14,18},{16,20},{1... | collective-permute-start | bytes 589832 | tf_op jit(solution)/shard_map/ppermute | solution.py:13
  332.3 13.8 %collective-permute-start.7 = (bf16[1,384,256]{2,1,0:T(8,128)(2,1)S(1)}, bf16[1,384,256]{2,1,0:T(8,128)(2,1)S(1)}, u32[]{:S(2)}, u32[]{:S(2)}) collective-permute-start(bf16[1,384,256]{2,1,0:T(8,128)(2,1)S(1)} %pad_maximum_fusion), channel_id=1, source_target_pairs={{4,0},{6,2},{8,4},{10,6},{12,8},{14,10},{16,12},{18,14},{20,16},{2... | collective-permute-start | bytes 589832 | tf_op jit(solution)/shard_map/ppermute | solution.py:13
  341.6 7.0 %collective-permute-start.6 = (bf16[1,384,256]{2,1,0:T(8,128)(2,1)S(1)}, bf16[1,384,256]{2,1,0:T(8,128)(2,1)S(1)}, u32[]{:S(2)}, u32[]{:S(2)}) collective-permute-start(bf16[1,384,256]{2,1,0:T(8,128)(2,1)S(1)} %pad_maximum_fusion), channel_id=1, source_target_pairs={{2,0},{4,2},{6,4},{8,6},{10,8},{12,10},{14,12},{16,14},{18,16},{20... | collective-permute-start | bytes 589832 | tf_op jit(solution)/shard_map/ppermute | solution.py:13
  349.1 16.1 %collective-permute-start.9 = (bf16[1,384,128]{2,1,0:T(8,128)(2,1)S(1)}, bf16[1,384,128]{2,1,0:T(8,128)(2,1)S(1)}, u32[]{:S(2)}, u32[]{:S(2)}) collective-permute-start(bf16[1,384,128]{2,1,0:T(8,128)(2,1)S(1)} %fusion.60), channel_id=1, source_target_pairs={{0,2},{2,4},{4,6},{6,8},{8,10},{10,12},{12,14},{14,16},{16,18},{18... | collective-permute-start | bytes 294920 | tf_op jit(solution)/shard_map/ppermute | solution.py:13
  351.2 14.2 %collective-permute-start.8 = (bf16[1,384,128]{2,1,0:T(8,128)(2,1)S(1)}, bf16[1,384,128]{2,1,0:T(8,128)(2,1)S(1)}, u32[]{:S(2)}, u32[]{:S(2)}) collective-permute-start(bf16[1,384,128]{2,1,0:T(8,128)(2,1)S(1)} %fusion.60), channel_id=1, source_target_pairs={{0,4},{2,6},{4,8},{6,10},{8,12},{10,14},{12,16},{14,18},{16,20},{1... | collective-permute-start | bytes 294920 | tf_op jit(solution)/shard_map/ppermute | solution.py:13
  353.1 12.4 %collective-permute-start.11 = (bf16[1,384,128]{2,1,0:T(8,128)(2,1)S(1)}, bf16[1,384,128]{2,1,0:T(8,128)(2,1)S(1)}, u32[]{:S(2)}, u32[]{:S(2)}) collective-permute-start(bf16[1,384,128]{2,1,0:T(8,128)(2,1)S(1)} %fusion.60), channel_id=1, source_target_pairs={{4,0},{6,2},{8,4},{10,6},{12,8},{14,10},{16,12},{18,14},{20,16},{2... | collective-permute-start | bytes 294920 | tf_op jit(solution)/shard_map/ppermute | solution.py:13
  362.2 5.9 %collective-permute-start.10 = (bf16[1,384,128]{2,1,0:T(8,128)(2,1)S(1)}, bf16[1,384,128]{2,1,0:T(8,128)(2,1)S(1)}, u32[]{:S(2)}, u32[]{:S(2)}) collective-permute-start(bf16[1,384,128]{2,1,0:T(8,128)(2,1)S(1)} %fusion.60), channel_id=1, source_target_pairs={{2,0},{4,2},{6,4},{8,6},{10,8},{12,10},{14,12},{16,14},{18,16},{20... | collective-permute-start | bytes 294920 | tf_op jit(solution)/shard_map/ppermute | solution.py:13
  370.3 16.1 %collective-permute-start.13 = (bf16[1,384,128]{2,1,0:T(8,128)(2,1)S(1)}, bf16[1,384,128]{2,1,0:T(8,128)(2,1)S(1)}, u32[]{:S(2)}, u32[]{:S(2)}) collective-permute-start(bf16[1,384,128]{2,1,0:T(8,128)(2,1)S(1)} %get-tuple-element.146), channel_id=1, source_target_pairs={{0,2},{2,4},{4,6},{6,8},{8,10},{10,12},{12,14},{14,16},{16,18},{18... | collective-permute-start | bytes 294920 | tf_op jit(solution)/shard_map/ppermute | solution.py:13
  372.5 14.2 %collective-permute-start.12 = (bf16[1,384,128]{2,1,0:T(8,128)(2,1)S(1)}, bf16[1,384,128]{2,1,0:T(8,128)(2,1)S(1)}, u32[]{:S(2)}, u32[]{:S(2)}) collective-permute-start(bf16[1,384,128]{2,1,0:T(8,128)(2,1)S(1)} %get-tuple-element.146), channel_id=1, source_target_pairs={{0,4},{2,6},{4,8},{6,10},{8,12},{10,14},{12,16},{14,18},{16,20},{1... | collective-permute-start | bytes 294920 | tf_op jit(solution)/shard_map/ppermute | solution.py:13
  374.4 12.5 %collective-permute-start.15 = (bf16[1,384,128]{2,1,0:T(8,128)(2,1)S(1)}, bf16[1,384,128]{2,1,0:T(8,128)(2,1)S(1)}, u32[]{:S(2)}, u32[]{:S(2)}) collective-permute-start(bf16[1,384,128]{2,1,0:T(8,128)(2,1)S(1)} %get-tuple-element.146), channel_id=1, source_target_pairs={{4,0},{6,2},{8,4},{10,6},{12,8},{14,10},{16,12},{18,14},{20,16},{2... | collective-permute-start | bytes 294920 | tf_op jit(solution)/shard_map/ppermute | solution.py:13
  383.5 5.9 %collective-permute-start.14 = (bf16[1,384,128]{2,1,0:T(8,128)(2,1)S(1)}, bf16[1,384,128]{2,1,0:T(8,128)(2,1)S(1)}, u32[]{:S(2)}, u32[]{:S(2)}) collective-permute-start(bf16[1,384,128]{2,1,0:T(8,128)(2,1)S(1)} %get-tuple-element.146), channel_id=1, source_target_pairs={{2,0},{4,2},{6,4},{8,6},{10,8},{12,10},{14,12},{16,14},{18,16},{20... | collective-permute-start | bytes 294920 | tf_op jit(solution)/shard_map/ppermute | solution.py:13
  389.7 16.1 %collective-permute-start.17 = (bf16[1,384,128]{2,1,0:T(8,128)(2,1)S(1)}, bf16[1,384,128]{2,1,0:T(8,128)(2,1)S(1)}, u32[]{:S(2)}, u32[]{:S(2)}) collective-permute-start(bf16[1,384,128]{2,1,0:T(8,128)(2,1)S(1)} %fusion.58), channel_id=1, source_target_pairs={{0,2},{2,4},{4,6},{6,8},{8,10},{10,12},{12,14},{14,16},{16,18},{18... | collective-permute-start | bytes 294920 | tf_op jit(solution)/shard_map/ppermute | solution.py:13
  391.8 14.2 %collective-permute-start.16 = (bf16[1,384,128]{2,1,0:T(8,128)(2,1)S(1)}, bf16[1,384,128]{2,1,0:T(8,128)(2,1)S(1)}, u32[]{:S(2)}, u32[]{:S(2)}) collective-permute-start(bf16[1,384,128]{2,1,0:T(8,128)(2,1)S(1)} %fusion.58), channel_id=1, source_target_pairs={{0,4},{2,6},{4,8},{6,10},{8,12},{10,14},{12,16},{14,18},{16,20},{1... | collective-permute-start | bytes 294920 | tf_op jit(solution)/shard_map/ppermute | solution.py:13
  393.7 12.4 %collective-permute-start.19 = (bf16[1,384,128]{2,1,0:T(8,128)(2,1)S(1)}, bf16[1,384,128]{2,1,0:T(8,128)(2,1)S(1)}, u32[]{:S(2)}, u32[]{:S(2)}) collective-permute-start(bf16[1,384,128]{2,1,0:T(8,128)(2,1)S(1)} %fusion.58), channel_id=1, source_target_pairs={{4,0},{6,2},{8,4},{10,6},{12,8},{14,10},{16,12},{18,14},{20,16},{2... | collective-permute-start | bytes 294920 | tf_op jit(solution)/shard_map/ppermute | solution.py:13
  402.8 5.9 %collective-permute-start.18 = (bf16[1,384,128]{2,1,0:T(8,128)(2,1)S(1)}, bf16[1,384,128]{2,1,0:T(8,128)(2,1)S(1)}, u32[]{:S(2)}, u32[]{:S(2)}) collective-permute-start(bf16[1,384,128]{2,1,0:T(8,128)(2,1)S(1)} %fusion.58), channel_id=1, source_target_pairs={{2,0},{4,2},{6,4},{8,6},{10,8},{12,10},{14,12},{16,14},{18,16},{20... | collective-permute-start | bytes 294920 | tf_op jit(solution)/shard_map/ppermute | solution.py:13
Sparse Core Ops, SparseCore 0:
  13.2 223.0 all-gather.2
where the time goes:
time: 418 us; the launch traced here: 416 us
  waiting for transfers between devices  234 us (56%)
  starting transfers between devices  80.5 us (19%)
  other arithmetic  40.6 us (10%)
  local copies, waits for them, and re-layouts  26.7 us (6%)
  matrix products  19.1 us (5%)
  between operations  14.7 us (4%)
    all_gather x1, waiting for transfers between devices, per_device(): arriving = lax.all_gather(strips, 'band', axis=0, tiled=True)  222 us
    ppermute x20, starting transfers between devices, passed_along(): return lax.ppermute(array, axis, pairs)  80.5 us
    dynamic_slice x32, local copies, waits for them, and re-layouts, per_device(): state, unused = lax.scan(advance, state, (blocks, starts))  25.9 us
    dot_general x50, matrix products, conv_valid(): jnp.dot(tap_slice.reshape(-1, tap_slice.shape[-1]), weight[kernel_tap], p...  12.6 us
    ppermute x20, waiting for transfers between devices, passed_along(): return lax.ppermute(array, axis, pairs)  11.3 us
    div x16, other arithmetic, strip_step(): row_centre = strip_row.astype(jnp.float32) / total_rows  10.4 us
    add x16, other arithmetic, strip_step(): strip_row = row_zero + jnp.arange(block_rows, dtype=jnp.int32)  10.3 us
  transfers between devices with their start and end apart: 21, of which 6 were waited for; matrix products, arithmetic and copies ran while one was open for 2% of the time, Pallas kernels for 0%

commit v1 on v0

--- a/solution.py
+++ b/solution.py
@@ -159,7 +159,15 @@
         zeros_state,
     )
     state = initial
-    arriving = lax.all_gather(strips, "band", axis=0, tiled=True)
+    arriving = jnp.concatenate(
+        lax.all_to_all(
+            jnp.stack(lax.axis_size("band") * [strips]),
+            axis_name="band",
+            split_axis=0,
+            concat_axis=0,
+        ),
+        axis=0,
+    )
     arriving_rows = arriving.shape[0]
     step_rows = min(arriving_rows, 16)
     full_steps = arriving_rows // step_rows

time: 418 us -> 481 us (1.15)
  waiting for transfers between devices: 234 us -> 280 us
  starting transfers between devices: 80.5 us -> 113 us
  between operations: 14.7 us -> 1.37 us
    all_to_all x0 -> x1, waiting for transfers between devices: none -> 268 us  [per_device(): lax.all_to_all(jnp.stack(lax.axis_size('band') * [strips]), axis_name='ba...]
    all_gather x1 -> x0, waiting for transfers between devices: 222 us -> none  [per_device(): arriving = lax.all_gather(strips, 'band', axis=0, tiled=True)]
    all_to_all x0 -> x1, starting transfers between devices: none -> 25.6 us  [per_device(): lax.all_to_all(jnp.stack(lax.axis_size('band') * [strips]), axis_name='ba...]
    ppermute x20, starting transfers between devices: 80.5 us -> 87 us  [passed_along(): return lax.ppermute(array, axis, pairs)]
  transfers between devices with their start and end apart: 21 -> 21, of which waited for: 6 -> 6; matrix products, arithmetic and copies ran while one was open for 2% -> 1% of each run, Pallas kernels for 0% -> 0%
where the time goes in v1:
time: 481 us; the launch traced here: 480 us
  waiting for transfers between devices  280 us (58%)
  starting transfers between devices  113 us (23%)
  other arithmetic  38.4 us (8%)
  local copies, waits for them, and re-layouts  29 us (6%)
  matrix products  17.3 us (4%)
    all_to_all x1, waiting for transfers between devices, per_device(): lax.all_to_all(jnp.stack(lax.axis_size('band') * [strips]), axis_name='ba...  268 us
    ppermute x20, starting transfers between devices, passed_along(): return lax.ppermute(array, axis, pairs)  87 us
    dynamic_slice x32, local copies, waits for them, and re-layouts, per_device(): state, unused = lax.scan(advance, state, (blocks, starts))  25.9 us
    all_to_all x1, starting transfers between devices, per_device(): lax.all_to_all(jnp.stack(lax.axis_size('band') * [strips]), axis_name='ba...  25.6 us
    ppermute x20, waiting for transfers between devices, passed_along(): return lax.ppermute(array, axis, pairs)  11.3 us
    dot_general x50, matrix products, conv_valid(): jnp.dot(tap_slice.reshape(-1, tap_slice.shape[-1]), weight[kernel_tap], p...  10.7 us
    div x16, other arithmetic, strip_step(): row_centre = strip_row.astype(jnp.float32) / total_rows  10.4 us
    add x16, other arithmetic, strip_step(): strip_row = row_zero + jnp.arange(block_rows, dtype=jnp.int32)  10.3 us
  transfers between devices with their start and end apart: 21, of which 6 were waited for; matrix products, arithmetic and copies ran while one was open for 1% of the time, Pallas kernels for 0%

profile of v1, /device:TPU:7, one launch (start us, length us, event | category | flops | bytes accessed | tf_op | source)
XLA Modules:
  0.0 479.6 jit_solution(16783379574916402410)
XLA Ops:
  0.6 1.0 convert_reduce_fusion
  1.7 3.1 stack.8
  4.8 25.6 %all-to-all-start = ((bf16[256,1,48,256]{3,2,1,0:T(8,128)(2,1)}), bf16[256,1,48,256]{3,2,1,0:T(8,128)(2,1)}, u32[]{:S(2)}, u32[]{:S(2)}) async-start(bf16[256,1,48,256]{3,2,1,0:T(8,128)(2,1)} %stack.8), calls=%async_computation | async-start | bytes 12582912 | tf_op jit(solution)/shard_map/all_to_all | solution.py:163
  31.3 268.3 %all-to-all-done = bf16[256,1,48,256]{3,2,1,0:T(8,128)(2,1)} async-done(((bf16[256,1,48,256]{3,2,1,0:T(8,128)(2,1)}), bf16[256,1,48,256]{3,2,1,0:T(8,128)(2,1)}, u32[]{:S(2)}, u32[]{:S(2)}) %all-to-all-start) | async-done | bytes 6291488 | tf_op jit(solution)/shard_map/all_to_all | solution.py:163
  299.7 70.1 %while.19 = (s32[]{:T(128)}, f32[384]{0:T(512)S(1)}, f32[384]{0:T(512)S(1)}, f32[384]{0:T(512)S(1)}, f32[384]{0:T(512)S(1)}, /*index=5*/f32[384]{0:T(512)S(1)}, ...) while((s32[]{:T(128)}, f32[384]{0:T(512)S(1)}, ...), condition=%wide.region_9.10_spmd.clone, body=%wide.region_1.9_spmd.clone.sunk | while | flops 153702400 | bytes 6978856 | solution.py:192
  299.7 1.1 constant_dynamic-slice_fusion.2
  303.2 0.7 convert_multiply_fusion.2
  304.1 1.0 constant_dynamic-slice_fusion.2
  308.5 1.0 constant_dynamic-slice_fusion.2
  312.8 1.0 constant_dynamic-slice_fusion.2
  317.2 1.0 constant_dynamic-slice_fusion.2
  321.6 1.0 constant_dynamic-slice_fusion.2
  326.0 1.0 constant_dynamic-slice_fusion.2
  330.4 1.0 constant_dynamic-slice_fusion.2
  334.7 1.0 constant_dynamic-slice_fusion.2
  339.1 1.0 constant_dynamic-slice_fusion.2
  343.5 1.0 constant_dynamic-slice_fusion.2
  347.9 1.0 constant_dynamic-slice_fusion.2
  352.2 1.0 constant_dynamic-slice_fusion.2
  356.6 1.0 constant_dynamic-slice_fusion.2
  361.0 1.0 constant_dynamic-slice_fusion.2
  365.4 1.0 constant_dynamic-slice_fusion.2
  372.6 9.8 %collective-permute-start.1 = (bf16[1,384,128]{2,1,0:T(8,128)(2,1)S(1)}, bf16[1,384,128]{2,1,0:T(8,128)(2,1)S(1)}, u32[]{:S(2)}, u32[]{:S(2)}) collective-permute-start(bf16[1,384,128]{2,1,0:T(8,128)(2,1)S(1)} %get-tuple-element.142), channel_id=1, source_target_pairs={{0,2},{2,4},{4,6},{6,8},{8,10},{10,12},{12,14},{14,16},{16,18},{18... | collective-permute-start | bytes 294920 | tf_op jit(solution)/shard_map/ppermute | solution.py:13
  382.4 1.9 collective-permute-start
  384.3 9.1 %collective-permute-start.3 = (bf16[1,384,128]{2,1,0:T(8,128)(2,1)S(1)}, bf16[1,384,128]{2,1,0:T(8,128)(2,1)S(1)}, u32[]{:S(2)}, u32[]{:S(2)}) collective-permute-start(bf16[1,384,128]{2,1,0:T(8,128)(2,1)S(1)} %get-tuple-element.142), channel_id=1, source_target_pairs={{4,0},{6,2},{8,4},{10,6},{12,8},{14,10},{16,12},{18,14},{20,16},{2... | collective-permute-start | bytes 294920 | tf_op jit(solution)/shard_map/ppermute | solution.py:13
  393.4 1.9 collective-permute-start.2
  395.4 3.6 collective-permute-start.5
  400.1 1.9 collective-permute-start.4
  402.2 9.1 %collective-permute-start.7 = (bf16[1,384,256]{2,1,0:T(8,128)(2,1)S(1)}, bf16[1,384,256]{2,1,0:T(8,128)(2,1)S(1)}, u32[]{:S(2)}, u32[]{:S(2)}) collective-permute-start(bf16[1,384,256]{2,1,0:T(8,128)(2,1)S(1)} %pad_maximum_fusion), channel_id=1, source_target_pairs={{4,0},{6,2},{8,4},{10,6},{12,8},{14,10},{16,12},{18,14},{20,16},{2... | collective-permute-start | bytes 589832 | tf_op jit(solution)/shard_map/ppermute | solution.py:13
  411.5 1.9 collective-permute-start.6
  414.2 1.8 collective-permute-done.7
  416.2 2.2 collective-permute-done.6
  419.1 1.9 collective-permute-start.9
  421.1 1.9 collective-permute-start.8
  423.1 9.1 %collective-permute-start.11 = (bf16[1,384,128]{2,1,0:T(8,128)(2,1)S(1)}, bf16[1,384,128]{2,1,0:T(8,128)(2,1)S(1)}, u32[]{:S(2)}, u32[]{:S(2)}) collective-permute-start(bf16[1,384,128]{2,1,0:T(8,128)(2,1)S(1)} %fusion.60), channel_id=1, source_target_pairs={{4,0},{6,2},{8,4},{10,6},{12,8},{14,10},{16,12},{18,14},{20,16},{2... | collective-permute-start | bytes 294920 | tf_op jit(solution)/shard_map/ppermute | solution.py:13
  432.2 3.0 collective-permute-start.10
  435.6 2.5 collective-permute-done.10
  440.3 1.9 collective-permute-start.13
  442.4 1.9 collective-permute-start.12
  444.3 9.1 %collective-permute-start.15 = (bf16[1,384,128]{2,1,0:T(8,128)(2,1)S(1)}, bf16[1,384,128]{2,1,0:T(8,128)(2,1)S(1)}, u32[]{:S(2)}, u32[]{:S(2)}) collective-permute-start(bf16[1,384,128]{2,1,0:T(8,128)(2,1)S(1)} %get-tuple-element.146), channel_id=1, source_target_pairs={{4,0},{6,2},{8,4},{10,6},{12,8},{14,10},{16,12},{18,14},{20,16},{2... | collective-permute-start | bytes 294920 | tf_op jit(solution)/shard_map/ppermute | solution.py:13
  453.4 3.0 collective-permute-start.14
  457.0 2.3 collective-permute-done.14
  459.6 1.9 collective-permute-start.17
  461.7 1.9 collective-permute-start.16
  463.7 9.1 %collective-permute-start.19 = (bf16[1,384,128]{2,1,0:T(8,128)(2,1)S(1)}, bf16[1,384,128]{2,1,0:T(8,128)(2,1)S(1)}, u32[]{:S(2)}, u32[]{:S(2)}) collective-permute-start(bf16[1,384,128]{2,1,0:T(8,128)(2,1)S(1)} %fusion.58), channel_id=1, source_target_pairs={{4,0},{6,2},{8,4},{10,6},{12,8},{14,10},{16,12},{18,14},{20,16},{2... | collective-permute-start | bytes 294920 | tf_op jit(solution)/shard_map/ppermute | solution.py:13
  472.8 3.0 collective-permute-start.18
  476.2 2.5 collective-permute-done.18
  478.7 0.9 multiply_add_fusion
  (369 shorter events, 62.7 us)
Async XLA Ops:
  4.8 25.7 %copy-start.6 = (f32[3,128]{1,0:T(4,128)S(1)}, f32[3,128]{1,0:T(4,128)}, u32[]{:S(2)}) copy-start(f32[3,128]{1,0:T(4,128)} %param.15) | copy-start | bytes 4612
  4.8 25.7 %copy-start.5 = (s32[2,1,384]{2,1,0:T(1,128)S(1)}, s32[2,1,384]{2,1,0:T(1,128)}, u32[]{:S(2)}) copy-start(s32[2,1,384]{2,1,0:T(1,128)} %param.14) | copy-start | bytes 9220
  4.8 25.7 %copy-start.1 = (bf16[1,384,128]{2,1,0:T(8,128)(2,1)S(1)}, bf16[1,384,128]{2,1,0:T(8,128)(2,1)}, u32[]{:S(2)}) copy-start(bf16[1,384,128]{2,1,0:T(8,128)(2,1)} %param.13) | copy-start | bytes 294916
  4.8 25.8 %copy-start.3 = (bf16[5,384,384]{2,1,0:T(8,128)(2,1)S(1)}, bf16[5,384,384]{2,1,0:T(8,128)(2,1)}, u32[]{:S(2)}) copy-start(bf16[5,384,384]{2,1,0:T(8,128)(2,1)} %param.16) | copy-start | bytes 4423684
  4.8 294.9 %all-to-all-start = ((bf16[256,1,48,256]{3,2,1,0:T(8,128)(2,1)}), bf16[256,1,48,256]{3,2,1,0:T(8,128)(2,1)}, u32[]{:S(2)}, u32[]{:S(2)}) async-start(bf16[256,1,48,256]{3,2,1,0:T(8,128)(2,1)} %stack.8), calls=%async_computation | async-start | bytes 12582912 | tf_op jit(solution)/shard_map/all_to_all | solution.py:163
  30.7 268.9 %copy-start = (bf16[1,384,256]{2,1,0:T(8,128)(2,1)S(1)}, bf16[1,384,256]{2,1,0:T(8,128)(2,1)}, u32[]{:S(2)}) copy-start(bf16[1,384,256]{2,1,0:T(8,128)(2,1)} %param.10) | copy-start | bytes 589828
  299.7 70.3 %copy-start.4 = (bf16[1,384,128]{2,1,0:T(8,128)(2,1)S(1)}, bf16[1,384,128]{2,1,0:T(8,128)(2,1)}, u32[]{:S(2)}) copy-start(bf16[1,384,128]{2,1,0:T(8,128)(2,1)} %param.12) | copy-start | bytes 294916
  371.7 27.3 %copy-start.2 = (bf16[5,384,384]{2,1,0:T(8,128)(2,1)S(1)}, bf16[5,384,384]{2,1,0:T(8,128)(2,1)}, u32[]{:S(2)}) copy-start(bf16[5,384,384]{2,1,0:T(8,128)(2,1)} %param.17) | copy-start | bytes 4423684
  372.6 27.5 %collective-permute-start.1 = (bf16[1,384,128]{2,1,0:T(8,128)(2,1)S(1)}, bf16[1,384,128]{2,1,0:T(8,128)(2,1)S(1)}, u32[]{:S(2)}, u32[]{:S(2)}) collective-permute-start(bf16[1,384,128]{2,1,0:T(8,128)(2,1)S(1)} %get-tuple-element.142), channel_id=1, source_target_pairs={{0,2},{2,4},{4,6},{6,8},{8,10},{10,12},{12,14},{14,16},{16,18},{18... | collective-permute-start | bytes 294920 | tf_op jit(solution)/shard_map/ppermute | solution.py:13
  382.4 19.8 %collective-permute-start = (bf16[1,384,128]{2,1,0:T(8,128)(2,1)S(1)}, bf16[1,384,128]{2,1,0:T(8,128)(2,1)S(1)}, u32[]{:S(2)}, u32[]{:S(2)}) collective-permute-start(bf16[1,384,128]{2,1,0:T(8,128)(2,1)S(1)} %get-tuple-element.142), channel_id=1, source_target_pairs={{0,4},{2,6},{4,8},{6,10},{8,12},{10,14},{12,16},{14,18},{16,20},{1... | collective-permute-start | bytes 294920 | tf_op jit(solution)/shard_map/ppermute | solution.py:13
  384.3 27.2 %collective-permute-start.3 = (bf16[1,384,128]{2,1,0:T(8,128)(2,1)S(1)}, bf16[1,384,128]{2,1,0:T(8,128)(2,1)S(1)}, u32[]{:S(2)}, u32[]{:S(2)}) collective-permute-start(bf16[1,384,128]{2,1,0:T(8,128)(2,1)S(1)} %get-tuple-element.142), channel_id=1, source_target_pairs={{4,0},{6,2},{8,4},{10,6},{12,8},{14,10},{16,12},{18,14},{20,16},{2... | collective-permute-start | bytes 294920 | tf_op jit(solution)/shard_map/ppermute | solution.py:13
  393.4 25.3 %collective-permute-start.2 = (bf16[1,384,128]{2,1,0:T(8,128)(2,1)S(1)}, bf16[1,384,128]{2,1,0:T(8,128)(2,1)S(1)}, u32[]{:S(2)}, u32[]{:S(2)}) collective-permute-start(bf16[1,384,128]{2,1,0:T(8,128)(2,1)S(1)} %get-tuple-element.142), channel_id=1, source_target_pairs={{2,0},{4,2},{6,4},{8,6},{10,8},{12,10},{14,12},{16,14},{18,16},{20... | collective-permute-start | bytes 294920 | tf_op jit(solution)/shard_map/ppermute | solution.py:13
  395.4 18.3 %collective-permute-start.5 = (bf16[1,384,256]{2,1,0:T(8,128)(2,1)S(1)}, bf16[1,384,256]{2,1,0:T(8,128)(2,1)S(1)}, u32[]{:S(2)}, u32[]{:S(2)}) collective-permute-start(bf16[1,384,256]{2,1,0:T(8,128)(2,1)S(1)} %pad_maximum_fusion), channel_id=1, source_target_pairs={{0,2},{2,4},{4,6},{6,8},{8,10},{10,12},{12,14},{14,16},{16,18},{18... | collective-permute-start | bytes 589832 | tf_op jit(solution)/shard_map/ppermute | solution.py:13
  400.1 13.8 %collective-permute-start.4 = (bf16[1,384,256]{2,1,0:T(8,128)(2,1)S(1)}, bf16[1,384,256]{2,1,0:T(8,128)(2,1)S(1)}, u32[]{:S(2)}, u32[]{:S(2)}) collective-permute-start(bf16[1,384,256]{2,1,0:T(8,128)(2,1)S(1)} %pad_maximum_fusion), channel_id=1, source_target_pairs={{0,4},{2,6},{4,8},{6,10},{8,12},{10,14},{12,16},{14,18},{16,20},{1... | collective-permute-start | bytes 589832 | tf_op jit(solution)/shard_map/ppermute | solution.py:13
  402.2 13.8 %collective-permute-start.7 = (bf16[1,384,256]{2,1,0:T(8,128)(2,1)S(1)}, bf16[1,384,256]{2,1,0:T(8,128)(2,1)S(1)}, u32[]{:S(2)}, u32[]{:S(2)}) collective-permute-start(bf16[1,384,256]{2,1,0:T(8,128)(2,1)S(1)} %pad_maximum_fusion), channel_id=1, source_target_pairs={{4,0},{6,2},{8,4},{10,6},{12,8},{14,10},{16,12},{18,14},{20,16},{2... | collective-permute-start | bytes 589832 | tf_op jit(solution)/shard_map/ppermute | solution.py:13
  411.5 7.0 %collective-permute-start.6 = (bf16[1,384,256]{2,1,0:T(8,128)(2,1)S(1)}, bf16[1,384,256]{2,1,0:T(8,128)(2,1)S(1)}, u32[]{:S(2)}, u32[]{:S(2)}) collective-permute-start(bf16[1,384,256]{2,1,0:T(8,128)(2,1)S(1)} %pad_maximum_fusion), channel_id=1, source_target_pairs={{2,0},{4,2},{6,4},{8,6},{10,8},{12,10},{14,12},{16,14},{18,16},{20... | collective-permute-start | bytes 589832 | tf_op jit(solution)/shard_map/ppermute | solution.py:13
  419.1 16.1 %collective-permute-start.9 = (bf16[1,384,128]{2,1,0:T(8,128)(2,1)S(1)}, bf16[1,384,128]{2,1,0:T(8,128)(2,1)S(1)}, u32[]{:S(2)}, u32[]{:S(2)}) collective-permute-start(bf16[1,384,128]{2,1,0:T(8,128)(2,1)S(1)} %fusion.60), channel_id=1, source_target_pairs={{0,2},{2,4},{4,6},{6,8},{8,10},{10,12},{12,14},{14,16},{16,18},{18... | collective-permute-start | bytes 294920 | tf_op jit(solution)/shard_map/ppermute | solution.py:13
  421.1 14.2 %collective-permute-start.8 = (bf16[1,384,128]{2,1,0:T(8,128)(2,1)S(1)}, bf16[1,384,128]{2,1,0:T(8,128)(2,1)S(1)}, u32[]{:S(2)}, u32[]{:S(2)}) collective-permute-start(bf16[1,384,128]{2,1,0:T(8,128)(2,1)S(1)} %fusion.60), channel_id=1, source_target_pairs={{0,4},{2,6},{4,8},{6,10},{8,12},{10,14},{12,16},{14,18},{16,20},{1... | collective-permute-start | bytes 294920 | tf_op jit(solution)/shard_map/ppermute | solution.py:13
  423.1 12.4 %collective-permute-start.11 = (bf16[1,384,128]{2,1,0:T(8,128)(2,1)S(1)}, bf16[1,384,128]{2,1,0:T(8,128)(2,1)S(1)}, u32[]{:S(2)}, u32[]{:S(2)}) collective-permute-start(bf16[1,384,128]{2,1,0:T(8,128)(2,1)S(1)} %fusion.60), channel_id=1, source_target_pairs={{4,0},{6,2},{8,4},{10,6},{12,8},{14,10},{16,12},{18,14},{20,16},{2... | collective-permute-start | bytes 294920 | tf_op jit(solution)/shard_map/ppermute | solution.py:13
  432.2 5.9 %collective-permute-start.10 = (bf16[1,384,128]{2,1,0:T(8,128)(2,1)S(1)}, bf16[1,384,128]{2,1,0:T(8,128)(2,1)S(1)}, u32[]{:S(2)}, u32[]{:S(2)}) collective-permute-start(bf16[1,384,128]{2,1,0:T(8,128)(2,1)S(1)} %fusion.60), channel_id=1, source_target_pairs={{2,0},{4,2},{6,4},{8,6},{10,8},{12,10},{14,12},{16,14},{18,16},{20... | collective-permute-start | bytes 294920 | tf_op jit(solution)/shard_map/ppermute | solution.py:13
  440.3 16.1 %collective-permute-start.13 = (bf16[1,384,128]{2,1,0:T(8,128)(2,1)S(1)}, bf16[1,384,128]{2,1,0:T(8,128)(2,1)S(1)}, u32[]{:S(2)}, u32[]{:S(2)}) collective-permute-start(bf16[1,384,128]{2,1,0:T(8,128)(2,1)S(1)} %get-tuple-element.146), channel_id=1, source_target_pairs={{0,2},{2,4},{4,6},{6,8},{8,10},{10,12},{12,14},{14,16},{16,18},{18... | collective-permute-start | bytes 294920 | tf_op jit(solution)/shard_map/ppermute | solution.py:13
  442.4 14.2 %collective-permute-start.12 = (bf16[1,384,128]{2,1,0:T(8,128)(2,1)S(1)}, bf16[1,384,128]{2,1,0:T(8,128)(2,1)S(1)}, u32[]{:S(2)}, u32[]{:S(2)}) collective-permute-start(bf16[1,384,128]{2,1,0:T(8,128)(2,1)S(1)} %get-tuple-element.146), channel_id=1, source_target_pairs={{0,4},{2,6},{4,8},{6,10},{8,12},{10,14},{12,16},{14,18},{16,20},{1... | collective-permute-start | bytes 294920 | tf_op jit(solution)/shard_map/ppermute | solution.py:13
  444.3 12.5 %collective-permute-start.15 = (bf16[1,384,128]{2,1,0:T(8,128)(2,1)S(1)}, bf16[1,384,128]{2,1,0:T(8,128)(2,1)S(1)}, u32[]{:S(2)}, u32[]{:S(2)}) collective-permute-start(bf16[1,384,128]{2,1,0:T(8,128)(2,1)S(1)} %get-tuple-element.146), channel_id=1, source_target_pairs={{4,0},{6,2},{8,4},{10,6},{12,8},{14,10},{16,12},{18,14},{20,16},{2... | collective-permute-start | bytes 294920 | tf_op jit(solution)/shard_map/ppermute | solution.py:13
  453.4 5.9 %collective-permute-start.14 = (bf16[1,384,128]{2,1,0:T(8,128)(2,1)S(1)}, bf16[1,384,128]{2,1,0:T(8,128)(2,1)S(1)}, u32[]{:S(2)}, u32[]{:S(2)}) collective-permute-start(bf16[1,384,128]{2,1,0:T(8,128)(2,1)S(1)} %get-tuple-element.146), channel_id=1, source_target_pairs={{2,0},{4,2},{6,4},{8,6},{10,8},{12,10},{14,12},{16,14},{18,16},{20... | collective-permute-start | bytes 294920 | tf_op jit(solution)/shard_map/ppermute | solution.py:13
  459.6 16.1 %collective-permute-start.17 = (bf16[1,384,128]{2,1,0:T(8,128)(2,1)S(1)}, bf16[1,384,128]{2,1,0:T(8,128)(2,1)S(1)}, u32[]{:S(2)}, u32[]{:S(2)}) collective-permute-start(bf16[1,384,128]{2,1,0:T(8,128)(2,1)S(1)} %fusion.58), channel_id=1, source_target_pairs={{0,2},{2,4},{4,6},{6,8},{8,10},{10,12},{12,14},{14,16},{16,18},{18... | collective-permute-start | bytes 294920 | tf_op jit(solution)/shard_map/ppermute | solution.py:13
  461.7 14.2 %collective-permute-start.16 = (bf16[1,384,128]{2,1,0:T(8,128)(2,1)S(1)}, bf16[1,384,128]{2,1,0:T(8,128)(2,1)S(1)}, u32[]{:S(2)}, u32[]{:S(2)}) collective-permute-start(bf16[1,384,128]{2,1,0:T(8,128)(2,1)S(1)} %fusion.58), channel_id=1, source_target_pairs={{0,4},{2,6},{4,8},{6,10},{8,12},{10,14},{12,16},{14,18},{16,20},{1... | collective-permute-start | bytes 294920 | tf_op jit(solution)/shard_map/ppermute | solution.py:13
  463.7 12.4 %collective-permute-start.19 = (bf16[1,384,128]{2,1,0:T(8,128)(2,1)S(1)}, bf16[1,384,128]{2,1,0:T(8,128)(2,1)S(1)}, u32[]{:S(2)}, u32[]{:S(2)}) collective-permute-start(bf16[1,384,128]{2,1,0:T(8,128)(2,1)S(1)} %fusion.58), channel_id=1, source_target_pairs={{4,0},{6,2},{8,4},{10,6},{12,8},{14,10},{16,12},{18,14},{20,16},{2... | collective-permute-start | bytes 294920 | tf_op jit(solution)/shard_map/ppermute | solution.py:13
  472.8 5.9 %collective-permute-start.18 = (bf16[1,384,128]{2,1,0:T(8,128)(2,1)S(1)}, bf16[1,384,128]{2,1,0:T(8,128)(2,1)S(1)}, u32[]{:S(2)}, u32[]{:S(2)}) collective-permute-start(bf16[1,384,128]{2,1,0:T(8,128)(2,1)S(1)} %fusion.58), channel_id=1, source_target_pairs={{2,0},{4,2},{6,4},{8,6},{10,8},{12,10},{14,12},{16,14},{18,16},{20... | collective-permute-start | bytes 294920 | tf_op jit(solution)/shard_map/ppermute | solution.py:13
